TPU v7x, 512 devices: a whole 4x8x8 slice. The times are simulated.
512 devices in a mesh: segment: 16 (over y, z_lo), ctx: 32 (over x, z_hi, core).
Axes of the slice: x: 4, y: 8, z: 8 (z_hi: 4, z_lo: 2; z = z_hi * 2 + z_lo), core: 2. Of those that a mesh axis runs over, the one named last changes fastest.
Arguments:
- perturbed_frame_activation: bfloat16 [2, 256, 1536], P(None, 'ctx'), may hold values from -8 to 8
- inbound_activation: bfloat16 [16, 256, 1536], P('segment', 'ctx'), may hold values from -6 to 6
- section_block_indices: int32 [16], P('segment'), may hold values from 1 to 2, as said below
- tile_arrival_permutation: int32 [2], replicated, may hold values from 0 to 1, each once
- adaptive_shifting: float32 [16, 2, 1536], P('segment'), may hold values from -6 to 6
- adaptive_scaling: float32 [16, 2, 1536], P('segment'), may hold values from -4 to 4
- tier_query_factor: float32 [16, 2, 1536], P('segment'), may hold values from 0.3 to 3
- tier_skip_coefficient: float32 [16, 2, 1536], P('segment'), may hold values from -12 to 12
- earlier_step_lookup_matrix: bfloat16 [16, 2, 2, 256, 1536], P('segment', None, None, 'ctx'), may hold values from -10.5 to 10.5
- earlier_step_content_matrix: bfloat16 [16, 2, 2, 256, 1536], P('segment', None, None, 'ctx'), may hold values from -3 to 3
Outputs:
- section_out: bfloat16 [16, 2, 256, 1536], P('segment', None, 'ctx')
Inputs may be any that keep to these rules, and one draw needn't show every extreme that they name: `section_block_indices`: some segment uses exactly 2 slots and some exactly 1. `tile_arrival_permutation`: each patch once.
All inputs are finite; a program needn't handle non-finite values.
Results may differ from a plain program's by a relative error of at most 0.013.
Values may be sent and summed in bfloat16 or wider, within the bound.
No kernel may reach another device: no remote copies, remote signals or barrier semaphores. Data moves between devices by JAX's collectives and lax.ppermute only.
A program may use at most 64 MiB of HBM per device.

v0:
```python
import math
import jax
import jax.numpy as jnp
from jax import lax
from jax.sharding import PartitionSpec as P

HD = 128
EPSILON = 1e-06


def head_norm(values):
    return values * lax.rsqrt(jnp.mean(values * values, axis=-1, keepdims=True) + EPSILON)


def per_device(
    perturbed_frame_activation,
    inbound_activation,
    section_block_indices,
    tile_arrival_permutation,
    adaptive_shifting,
    adaptive_scaling,
    tier_query_factor,
    tier_skip_coefficient,
    earlier_step_lookup_matrix,
    earlier_step_content_matrix,
):
    segment = lax.axis_index("segment")
    place = lax.axis_index("ctx")
    patch_count = tile_arrival_permutation.shape[0]
    rows = inbound_activation.shape[1]
    width = inbound_activation.shape[2]
    heads = width // HD
    slot_count = earlier_step_lookup_matrix.shape[1]
    layers_here = section_block_indices[0]
    scale = 1.0 / math.sqrt(HD)

    def pick_patch(stack, patch, axis):
        return lax.dynamic_index_in_dim(stack, patch, axis, keepdims=False)

    first_rows = jnp.where(
        segment == 0,
        pick_patch(perturbed_frame_activation, tile_arrival_permutation[0], 0),
        inbound_activation[0],
    )
    entry_rows = [first_rows[None]]
    for turn in range(1, patch_count):
        entry_rows.append(
            pick_patch(perturbed_frame_activation, tile_arrival_permutation[turn], 0)[None]
        )
    other_patch = tile_arrival_permutation[jnp.mod(1 - segment, patch_count)]
    far_k = pick_patch(earlier_step_lookup_matrix[0], other_patch, 1)
    far_v = pick_patch(earlier_step_content_matrix[0], other_patch, 1)
    packed = jnp.concatenate(entry_rows + [far_k, far_v], axis=0)
    whole = lax.all_gather(packed, "ctx", axis=1, tiled=True)
    entry = whole[:patch_count]
    far_k = whole[patch_count : patch_count + slot_count]
    far_v = whole[patch_count + slot_count :]
    tokens = whole.shape[1]

    def layer(state, tier, keys_far, values_far):
        live = layers_here > tier
        x = state.astype(jnp.float32)
        hidden = (
            x
            * lax.rsqrt(jnp.mean(x * x, axis=-1, keepdims=True) + EPSILON)
            * (1.0 + adaptive_scaling[0, tier])
            + adaptive_shifting[0, tier]
        )
        query = head_norm(hidden.reshape(tokens, heads, HD)).astype(jnp.bfloat16)
        fresh_key = head_norm(
            (hidden * tier_query_factor[0, tier]).reshape(tokens, heads, HD)
        ).astype(jnp.bfloat16)
        fresh_value = hidden.astype(jnp.bfloat16).reshape(tokens, heads, HD)
        keys = jnp.concatenate([fresh_key, keys_far.reshape(tokens, heads, HD)], axis=0)
        values = jnp.concatenate([fresh_value, values_far.reshape(tokens, heads, HD)], axis=0)
        scores = jnp.einsum("phd,nhd->phn", query, keys, preferred_element_type=jnp.float32) * scale
        weights = jnp.exp(scores)
        total = jnp.sum(weights, axis=-1)
        numerator = jnp.einsum(
            "phn,nhd->phd", weights.astype(jnp.bfloat16), values, preferred_element_type=jnp.float32
        )
        attended = (numerator / total[..., None]).reshape(tokens, width)
        new_state = (x + tier_skip_coefficient[0, tier] * attended).astype(jnp.bfloat16)
        return (
            jnp.where(live, new_state, state),
            fresh_key.reshape(tokens, width),
            fresh_value.reshape(tokens, width),
        )

    def own_rows(state):
        return lax.dynamic_slice_in_dim(state, place * rows, rows, 0)

    outcomes = []
    state = entry[0]
    turn_zero_kv = []
    for tier in range(slot_count):
        state, fresh_key, fresh_value = layer(state, tier, far_k[tier], far_v[tier])
        turn_zero_kv.append((fresh_key, fresh_value))
    outcomes.append(own_rows(state))
    count = lax.axis_size("segment")
    for turn in range(1, patch_count):
        arrived = lax.ppermute(state, "segment", [(i, i + 1) for i in range(count - 1)])
        state = jnp.where(segment == 0, entry[turn], arrived)
        for tier in range(slot_count):
            state, _, _ = layer(state, tier, *turn_zero_kv[tier])
        outcomes.append(own_rows(state))
    return jnp.stack(outcomes)[None]


def solution(mesh):
    return jax.shard_map(
        per_device,
        mesh=mesh,
        in_specs=(
            P(None, "ctx", None),
            P("segment", "ctx", None),
            P("segment"),
            P(),
            P("segment", None, None),
            P("segment", None, None),
            P("segment", None, None),
            P("segment", None, None),
            P("segment", None, None, "ctx", None),
            P("segment", None, None, "ctx", None),
        ),
        out_specs=P("segment", None, "ctx", None),
        check_vma=False,
    )
```

profile of v0, /device:TPU:32, one launch (start us, length us, event | category | flops | bytes accessed | tf_op | source)
XLA Modules:
  0.0 188.3 jit_solution(44315173992806719)
XLA Ops:
  6.5 1.4 fusion.106
  13.7 0.8 dynamic-slice_bitcast_fusion
  14.5 0.8 dynamic-slice_select_fusion
  15.3 0.7 pad_maximum_fusion
  16.6 0.8 slice_reduce_fusion.2
  17.5 0.8 add_reduce_fusion
  18.3 0.9 slice_reduce_fusion
  19.1 70.0 %all-gather.2.cloned.1.call-done = bf16[6,256,1536]{2,1,0:T(8,128)(2,1)} async-done(((bf16[6,8,1536]{2,1,0:T(8,128)(2,1)}), bf16[6,256,1536]{2,1,0:T(8,128)(2,1)}) %all-gather.2.cloned.1.call-update) | async-done | bytes 4718608 | tf_op jit(solution)/shard_map/all_gather | solution.py:54
  89.1 1.4 fusion.8
  90.5 3.5 %fusion.105 = (bf16[1,256,1536]{2,1,0:T(8,128)(2,1)}, bf16[1,256,1536]{2,1,0:T(8,128)(2,1)}, bf16[1,256,1536]{2,1,0:T(8,128)(2,1)S(1)}, bf16[1,256,1536]{2,1,0:T(8,128)(2,1)S(1)}, bf16[1,256,1536]{2,1,0:T(8,128)(2,1)S(1)}) fusion(bf16[6,256,1536]{2,1,0:T(8,128)(2,1)} %all-gather.2.cloned.1.call-done), kind=kLoop, calls=%fused_computation.164 | loop fusion | bytes 7864320 | tf_op jit(solution)/shard_map/slice | solution.py:97
  94.0 1.4 copy.38
  95.4 1.2 copy.39
  96.6 1.4 copy.40
  98.0 1.2 copy.41
  99.4 1.2 copy.31
  102.0 1.0 fusion.20
  103.6 1.5 bitcast_reduce_fusion.3
  105.1 2.0 %bitcast_divide_fusion.3 = f32[256,12,128]{2,0,1:T(8,128)S(1)} fusion(f32[12,512,256]{2,1,0:T(8,128)S(1)} %get-tuple-element.43, bf16[256,12,128]{2,0,1:T(8,128)(2,1)S(1)} %copy.29, bf16[256,12,128]{2,0,1:T(8,128)(2,1)S(1)} %get-tuple-element.36, f32[256,12]{0,1:T(8,128)S(1)} %get-tuple-element.42), kind=kOutput, calls=%fused_computation.81 | convolution fusion | flops 409337856 | bytes 9449472 | tf_op jit(solution)/shard_map/phn,nhd->phd/dot_general | solution.py:79
  107.1 1.6 copy.35
  108.7 3.0 %copy.36 = f32[256,1536]{1,0:T(8,128)} copy(f32[256,1536]{0,1:T(8,128)} %bitcast.90) | data formatting | bytes 3145728 | tf_op jit(solution)/shard_map/reshape | solution.py:82
  111.7 2.0 %fusion.23 = (f32[256]{0:T(256)S(1)}, bf16[256,1536]{1,0:T(8,128)(2,1)S(1)}) fusion(f32[256,1536]{1,0:T(8,128)} %copy.36, f32[1536]{0:T(1024)S(1)} %get-tuple-element.10, bf16[6,256,1536]{2,1,0:T(8,128)(2,1)} %all-gather.2.cloned.1.call-done, pred[]{:T(512)} %bitcast.1), kind=kLoop, calls=%fused_computation.44 | loop fusion | flops 3145472 | bytes 3152897 | tf_op jit(solution)/shard_map/reduce_sum | solution.py:65
  114.3 1.0 multiply_reduce_fusion.5
  115.9 1.4 bitcast_reduce_fusion.2
  117.3 2.3 %bitcast_divide_fusion.2 = f32[256,12,128]{0,2,1:T(8,128)} fusion(f32[12,512,256]{2,1,0:T(8,128)S(1)} %get-tuple-element.45, bf16[256,12,128]{2,0,1:T(8,128)(2,1)S(1)} %copy-done.6, bf16[256,12,128]{2,0,1:T(8,128)(2,1)S(1)} %get-tuple-element.21, f32[256,12]{0,1:T(8,128)S(1)} %get-tuple-element.44), kind=kOutput, calls=%fused_computation.80 | convolution fusion | flops 409337856 | bytes 9449472 | tf_op jit(solution)/shard_map/phn,nhd->phd/dot_general | solution.py:79
  119.7 1.9 copy.44
  121.8 2.8 %collective-permute-start = (bf16[256,1536]{1,0:T(8,128)(2,1)S(1)}, bf16[256,1536]{1,0:T(8,128)(2,1)S(1)}, u32[]{:S(2)}, u32[]{:S(2)}) collective-permute-start(bf16[256,1536]{1,0:T(8,128)(2,1)S(1)} %fusion.68), channel_id=1, source_target_pairs={{0,32},{32,64},{64,96},{96,128},{128,160},{160,192},{192,224},{224... | collective-permute-start | bytes 2359304 | tf_op jit(solution)/shard_map/ppermute | solution.py:102
  124.6 20.9 %collective-permute-done = bf16[256,1536]{1,0:T(8,128)(2,1)S(1)} collective-permute-done((bf16[256,1536]{1,0:T(8,128)(2,1)S(1)}, bf16[256,1536]{1,0:T(8,128)(2,1)S(1)}, u32[]{:S(2)}, u32[]{:S(2)}) %collective-permute-start) | collective-permute-done | bytes 786464 | tf_op jit(solution)/shard_map/ppermute | solution.py:102
  145.5 1.5 fusion.25
  147.0 2.2 %fusion.99 = (bf16[256,1536]{1,0:T(8,128)(2,1)}, f32[256,1536]{1,0:T(8,128)}, f32[256,1536]{1,0:T(8,128)}) fusion(f32[1536]{0:T(1024)S(1)} %get-tuple-element.52, f32[1536]{0:T(1024)S(1)} %get-tuple-element.12, f32[256]{0:T(256)S(1)} %add_rsqrt_fusion.9, bf16[256,1536]{1,0:T(8,128)(2,1)S(1)} %get-tuple-element.20, f32[1536]{0:T(1024)S(1)} %get-tuple-element.16), kind=kLoop, calls=%fused_computation.162 | loop fusion | flops 2359296 | bytes 4738048 | tf_op jit(solution)/shard_map/convert_element_type | solution.py:73
  149.3 1.9 copy.47
  151.3 1.6 copy.48
  152.9 1.4 copy.45
  154.3 1.2 copy.46
  155.5 1.9 copy.49
  157.5 1.2 copy-done
  159.3 1.5 bitcast_reduce_fusion.1
  160.8 2.3 %bitcast_divide_fusion.1 = f32[256,12,128]{0,2,1:T(8,128)} fusion(f32[12,512,256]{2,1,0:T(8,128)S(1)} %get-tuple-element.47, bf16[256,12,128]{2,0,1:T(8,128)(2,1)S(1)} %copy-done.13, bf16[256,12,128]{2,0,1:T(8,128)(2,1)S(1)} %copy-done.9, f32[256,12]{0,1:T(8,128)S(1)} %get-tuple-element.46), kind=kOutput, calls=%fused_computation.79 | convolution fusion | flops 409337856 | bytes 9449472 | tf_op jit(solution)/shard_map/phn,nhd->phd/dot_general | solution.py:79
  163.1 1.9 copy.53
  165.0 1.4 fusion.100
  166.7 2.0 %fusion.98 = (bf16[256,1536]{1,0:T(8,128)(2,1)S(1)}, f32[256,1536]{1,0:T(8,128)}, f32[256,1536]{1,0:T(8,128)}) fusion(f32[1536]{0:T(1024)S(1)} %get-tuple-element.53, f32[1536]{0:T(1024)S(1)} %get-tuple-element.11, f32[256]{0:T(256)S(1)} %add_rsqrt_fusion.8, bf16[256,1536]{1,0:T(8,128)(2,1)S(1)} %get-tuple-element.18, f32[1536]{0:T(1024)S(1)} %get-tuple-element.15), kind=kLoop, calls=%fused_computation.161 | loop fusion | flops 2359296 | bytes 4738048 | tf_op jit(solution)/shard_map/convert_element_type | solution.py:73
  168.7 1.9 copy.56
  170.7 1.6 copy.57
  173.0 1.9 copy.58
  175.1 1.2 copy-done.1
  176.8 1.3 bitcast_reduce_fusion
  178.1 1.4 bitcast_divide_fusion
  180.0 0.8 fusion.85
  180.8 0.6 maximum_bitcast_fusion
  (61 shorter events, 6.4 us)
Async XLA Ops:
  6.5 82.6 %all-gather.2.cloned.1.call-start = ((), (), s32[]{:S(2)}) async-start(), calls=%async_computation | async-start | bytes 4866048 | tf_op jit(solution)/shard_map/all_gather | solution.py:54
  102.0 1.6 copy-start.8
  103.0 2.1 %copy-start.12 = (bf16[256,12,128]{2,0,1:T(8,128)(2,1)}, bf16[256,12,128]{2,0,1:T(8,128)(2,1)S(1)}, u32[]{:S(2)}) copy-start(bf16[256,12,128]{2,0,1:T(8,128)(2,1)S(1)} %get-tuple-element.36) | copy-start | bytes 2359300
  103.6 1.5 copy-start.4
  114.3 3.0 %copy-start.10 = (bf16[256,12,128]{2,0,1:T(8,128)(2,1)}, bf16[256,12,128]{2,0,1:T(8,128)(2,1)S(1)}, u32[]{:S(2)}) copy-start(bf16[256,12,128]{2,0,1:T(8,128)(2,1)S(1)} %get-tuple-element.21) | copy-start | bytes 2359300
  114.3 1.6 copy-start.7
  115.9 1.4 copy-start.2
  115.9 1.4 copy-start.6
  121.8 23.7 %collective-permute-start = (bf16[256,1536]{1,0:T(8,128)(2,1)S(1)}, bf16[256,1536]{1,0:T(8,128)(2,1)S(1)}, u32[]{:S(2)}, u32[]{:S(2)}) collective-permute-start(bf16[256,1536]{1,0:T(8,128)(2,1)S(1)} %fusion.68), channel_id=1, source_target_pairs={{0,32},{32,64},{64,96},{96,128},{128,160},{160,192},{192,224},{224... | collective-permute-start | bytes 2359304 | tf_op jit(solution)/shard_map/ppermute | solution.py:102
  157.4 1.4 copy-start
  157.5 1.7 copy-start.5
  159.3 1.5 copy-start.9
  159.3 1.5 copy-start.13
  174.9 1.4 copy-start.1
  175.0 1.7 copy-start.3
  176.8 1.3 copy-start.11
Sparse Core Ops, SparseCore 0:
  16.1 72.9 all-gather.1
where the time goes:
time: 189 us; the launch traced here: 188 us
  waiting for transfers between devices  90.9 us (48%)
  local copies, waits for them, and re-layouts  40.8 us (22%)
  between operations  20.3 us (11%)
  other arithmetic  19.9 us (11%)
  matrix products  13.6 us (7%)
  starting transfers between devices  2.77 us (1%)
    all_gather x1, waiting for transfers between devices, per_device(): whole = lax.all_gather(packed, 'ctx', axis=1, tiled=True)  70 us
    ppermute x1, waiting for transfers between devices, per_device(): lax.ppermute(state, 'segment', [(i, i + 1) for i in range(count - 1)])  20.9 us
    dot_general x4, matrix products, layer(): jnp.einsum('phn,nhd->phd', weights.astype(jnp.bfloat16), values, preferre...  7.99 us
    slice x5, local copies, waits for them, and re-layouts, per_device(): state, fresh_key, fresh_value = layer(state, tier, far_k[tier], far_v[tier])  6.85 us
    reshape x3, local copies, waits for them, and re-layouts, layer(): attended = (numerator / total[..., None]).reshape(tokens, width)  6.77 us
    dot_general x4, matrix products, layer(): jnp.einsum('phd,nhd->phn', query, keys, preferred_element_type=jnp.float32)  5.65 us
    reduce_sum x4, other arithmetic, layer(): jnp.mean(x * x, axis=-1, keepdims=True) + EPSILON  5.12 us
    convert_element_type x3, other arithmetic, layer(): fresh_value = hidden.astype(jnp.bfloat16).reshape(tokens, heads, HD)  4.79 us
  transfers between devices with their start and end apart: 2, of which 2 were waited for; matrix products, arithmetic and copies ran while one was open for 1% of the time, Pallas kernels for 0%

commit v1 on v0

--- a/solution.py
+++ b/solution.py
@@ -51,7 +51,10 @@
     far_k = pick_patch(earlier_step_lookup_matrix[0], other_patch, 1)
     far_v = pick_patch(earlier_step_content_matrix[0], other_patch, 1)
     packed = jnp.concatenate(entry_rows + [far_k, far_v], axis=0)
-    whole = lax.all_gather(packed, "ctx", axis=1, tiled=True)
+    devices = lax.axis_size("ctx")
+    parts = jnp.stack([packed for _ in range(devices)])
+    parts = lax.all_to_all(parts, "ctx", split_axis=0, concat_axis=0)
+    whole = jnp.concatenate(parts, axis=1)
     entry = whole[:patch_count]
     far_k = whole[patch_count : patch_count + slot_count]
     far_v = whole[patch_count + slot_count :]

time: 189 us -> 241 us (1.28)
  the two profiles are of different devices: /device:TPU:32 before, /device:TPU:41 now
where the time goes in v1:
time: 241 us; the launch traced here: 240 us
  waiting for transfers between devices  101 us (42%)
  local copies, waits for them, and re-layouts  56.3 us (23%)
  starting transfers between devices  42.2 us (18%)
  other arithmetic  20 us (8%)
  matrix products  13.4 us (6%)
  between operations  6.92 us (3%)
    all_to_all x1, waiting for transfers between devices, per_device(): parts = lax.all_to_all(parts, 'ctx', split_axis=0, concat_axis=0)  83.1 us
    ppermute x1, starting transfers between devices, per_device(): lax.ppermute(state, 'segment', [(i, i + 1) for i in range(count - 1)])  28.4 us
    ppermute x1, waiting for transfers between devices, per_device(): lax.ppermute(state, 'segment', [(i, i + 1) for i in range(count - 1)])  18.1 us
    all_to_all x1, starting transfers between devices, per_device(): parts = lax.all_to_all(parts, 'ctx', split_axis=0, concat_axis=0)  13.8 us
    reshape x4, local copies, waits for them, and re-layouts, layer(): attended = (numerator / total[..., None]).reshape(tokens, width)  9.56 us
    dot_general x4, matrix products, layer(): jnp.einsum('phn,nhd->phd', weights.astype(jnp.bfloat16), values, preferre...  7.8 us
    another operation x4, local copies, waits for them, and re-layouts, layer(): values_far.reshape(tokens, heads, HD)  6.66 us
    another operation x4, local copies, waits for them, and re-layouts, layer(): keys_far.reshape(tokens, heads, HD)  6.1 us
  transfers between devices with their start and end apart: 2, of which 2 were waited for; matrix products, arithmetic and copies ran while one was open for 0% of the time, Pallas kernels for 0%

profile of v1, /device:TPU:41, one launch (start us, length us, event | category | flops | bytes accessed | tf_op | source)
XLA Modules:
  0.0 240.0 jit_solution(11342831954980718103)
XLA Ops:
  0.0 1.4 fusion.105
  8.8 2.7 %stack.8 = bf16[32,6,8,1536]{3,2,1,0:T(8,128)(2,1)} broadcast(bf16[6,8,1536]{2,1,0:T(8,128)(2,1)S(1)} %pad_maximum_fusion), dimensions={1,2,3} | broadcast | bytes 4866048 | tf_op jit(solution)/shard_map/stack | solution.py:55
  11.5 13.8 %all-to-all-start = ((bf16[32,6,8,1536]{3,2,1,0:T(8,128)(2,1)}), bf16[32,6,8,1536]{3,2,1,0:T(8,128)(2,1)}, u32[]{:S(2)}, u32[]{:S(2)}) async-start(bf16[32,6,8,1536]{3,2,1,0:T(8,128)(2,1)} %stack.8), calls=%async_computation | async-start | bytes 9437184 | tf_op jit(solution)/shard_map/all_to_all | solution.py:56
  26.1 83.1 %all-to-all-done = bf16[32,6,8,1536]{3,2,1,0:T(8,128)(2,1)} async-done(((bf16[32,6,8,1536]{3,2,1,0:T(8,128)(2,1)}), bf16[32,6,8,1536]{3,2,1,0:T(8,128)(2,1)}, u32[]{:S(2)}, u32[]{:S(2)}) %all-to-all-start) | async-done | bytes 4718624 | tf_op jit(solution)/shard_map/all_to_all | solution.py:56
  109.2 2.7 %copy.122 = bf16[32,6,8,1536]{3,2,0,1:T(8,128)(2,1)S(1)} copy(bf16[32,6,8,1536]{3,2,1,0:T(8,128)(2,1)} %all-to-all-done) | data formatting | bytes 9437184 | tf_op jit(solution)/shard_map/all_to_all | solution.py:56
  112.2 2.0 fusion.104
  115.7 1.4 fusion.18
  117.6 1.9 reshape_squeeze.13
  119.5 1.1 copy.64
  120.7 1.6 reshape_squeeze.12
  122.5 0.9 copy-done.12
  123.5 1.5 bitcast_reduce_fusion.3
  124.9 1.8 bitcast_divide_fusion.3
  126.7 1.6 copy.68
  128.3 2.3 copy.71
  130.7 2.5 %reshape_squeeze.14 = bf16[256,12,128]{2,1,0:T(8,128)(2,1)} reshape(bf16[1,32,8,1536]{3,2,1,0:T(8,128)(2,1)} %get-tuple-element.23) | data formatting | bytes 1572864 | tf_op jit(solution)/shard_map/reshape;squeeze | solution.py:78
  133.2 2.3 copy.72
  135.5 1.6 reshape_squeeze.15
  137.1 1.4 copy.73
  138.5 3.1 %copy.69 = f32[256,1536]{1,0:T(8,128)} copy(f32[256,1536]{0,1:T(8,128)} %bitcast.101) | data formatting | bytes 3145728 | tf_op jit(solution)/shard_map/reshape | solution.py:85
  141.6 2.6 %reshape.370 = f32[1,32,8,1536]{3,2,1,0:T(8,128)} reshape(f32[256,12,128]{2,1,0:T(8,128)} %copy.71) | data formatting | bytes 3145728 | tf_op jit(solution)/shard_map/reshape | solution.py:85
  144.2 2.0 multiply_reduce_fusion.7
  146.9 1.0 multiply_reduce_fusion.5
  148.5 1.4 bitcast_reduce_fusion.2
  149.9 2.3 bitcast_divide_fusion.2
  152.2 2.0 copy.76
  154.3 2.5 %fusion.66 = bf16[256,1536]{1,0:T(8,128)(2,1)} fusion(f32[256,1536]{1,0:T(8,128)S(1)} %copy.76, f32[256,1536]{1,0:T(8,128)S(1)} %copy-done.3, f32[1536]{0:T(1024)S(1)} %get-tuple-element.9, f32[1536]{0:T(1024)S(1)} %get-tuple-element.10, pred[]{:T(512)} %bitcast.1, pred[]{:T(512)} %bitcast, bf16[6,32,8,1536]{3,2,1,0:T(8,128)(2,1)} %bitcast.91), kind=kLoop, calls=%fused_computation.100 | loop fusion | flops 3932160 | bytes 4730882 | tf_op jit(solution)/shard_map/jit(_where)/select_n | solution.py:88
  156.7 28.4 %collective-permute-start = (bf16[256,1536]{1,0:T(8,128)(2,1)}, bf16[256,1536]{1,0:T(8,128)(2,1)S(1)}, u32[]{:S(2)}, u32[]{:S(2)}) collective-permute-start(bf16[256,1536]{1,0:T(8,128)(2,1)} %fusion.66), channel_id=1, source_target_pairs={{0,32},{32,64},{64,96},{96,128},{128,160},{160,192},{192,224},{224... | collective-permute-start | bytes 2359304 | tf_op jit(solution)/shard_map/ppermute | solution.py:105
  185.9 18.1 %collective-permute-done = bf16[256,1536]{1,0:T(8,128)(2,1)S(1)} collective-permute-done((bf16[256,1536]{1,0:T(8,128)(2,1)}, bf16[256,1536]{1,0:T(8,128)(2,1)S(1)}, u32[]{:S(2)}, u32[]{:S(2)}) %collective-permute-start) | collective-permute-done | bytes 786464 | tf_op jit(solution)/shard_map/ppermute | solution.py:105
  204.0 1.5 fusion.23
  205.5 2.4 fusion.99
  207.8 1.9 copy.79
  209.8 1.6 copy.80
  211.4 1.4 copy.77
  212.8 1.2 copy.78
  214.1 1.9 copy.81
  216.1 1.2 copy-done.1
  217.9 1.5 bitcast_reduce_fusion.1
  219.4 2.3 bitcast_divide_fusion.1
  221.7 1.9 copy.85
  223.6 1.4 fusion.100
  225.3 2.0 fusion.98
  227.3 1.9 copy.88
  229.3 1.6 copy.89
  231.6 1.9 copy.90
  233.6 1.2 copy-done.2
  235.4 1.3 bitcast_reduce_fusion
  236.7 1.4 bitcast_divide_fusion
  (77 shorter events, 10.6 us)
Async XLA Ops:
  11.5 14.5 %copy-start.16 = (f32[1,2,1536]{2,1,0:T(2,128)S(1)}, f32[1,2,1536]{2,1,0:T(2,128)}, u32[]{:S(2)}) copy-start(f32[1,2,1536]{2,1,0:T(2,128)} %param.17) | copy-start | bytes 36868
  11.5 14.5 %copy-start.17 = (f32[1,2,1536]{2,1,0:T(2,128)S(1)}, f32[1,2,1536]{2,1,0:T(2,128)}, u32[]{:S(2)}) copy-start(f32[1,2,1536]{2,1,0:T(2,128)} %param.15) | copy-start | bytes 36868
  11.5 14.6 %copy-start.18 = (f32[1,2,1536]{2,1,0:T(2,128)S(1)}, f32[1,2,1536]{2,1,0:T(2,128)}, u32[]{:S(2)}) copy-start(f32[1,2,1536]{2,1,0:T(2,128)} %param.16) | copy-start | bytes 36868
  11.5 14.6 %copy-start.19 = (f32[1,2,1536]{2,1,0:T(2,128)S(1)}, f32[1,2,1536]{2,1,0:T(2,128)}, u32[]{:S(2)}) copy-start(f32[1,2,1536]{2,1,0:T(2,128)} %param.14) | copy-start | bytes 36868
  11.5 97.7 %all-to-all-start = ((bf16[32,6,8,1536]{3,2,1,0:T(8,128)(2,1)}), bf16[32,6,8,1536]{3,2,1,0:T(8,128)(2,1)}, u32[]{:S(2)}, u32[]{:S(2)}) async-start(bf16[32,6,8,1536]{3,2,1,0:T(8,128)(2,1)} %stack.8), calls=%async_computation | async-start | bytes 9437184 | tf_op jit(solution)/shard_map/all_to_all | solution.py:56
  111.9 3.1 %copy-start = (bf16[32,6,8,1536]{3,2,0,1:T(8,128)(2,1)}, bf16[32,6,8,1536]{3,2,0,1:T(8,128)(2,1)S(1)}, u32[]{:S(2)}) copy-start(bf16[32,6,8,1536]{3,2,0,1:T(8,128)(2,1)S(1)} %copy.122) | copy-start | bytes 14155780
  117.6 4.9 %copy-start.4 = (bf16[256,12,128]{2,0,1:T(8,128)(2,1)}, bf16[256,12,128]{2,0,1:T(8,128)(2,1)S(1)}, u32[]{:S(2)}) copy-start(bf16[256,12,128]{2,0,1:T(8,128)(2,1)S(1)} %fusion.17) | copy-start | bytes 2359300
  122.3 1.1 copy-start.12
  123.5 1.5 copy-start.13
  130.6 4.8 %copy-start.8 = (bf16[1,32,8,1536]{3,2,1,0:T(8,128)(2,1)S(1)}, bf16[1,32,8,1536]{3,2,1,0:T(8,128)(2,1)}, u32[]{:S(2)}) copy-start(bf16[1,32,8,1536]{3,2,1,0:T(8,128)(2,1)} %get-tuple-element.24) | copy-start | bytes 2359300
  146.9 3.0 %copy-start.9 = (bf16[256,12,128]{2,0,1:T(8,128)(2,1)}, bf16[256,12,128]{2,0,1:T(8,128)(2,1)S(1)}, u32[]{:S(2)}) copy-start(bf16[256,12,128]{2,0,1:T(8,128)(2,1)S(1)} %get-tuple-element.21) | copy-start | bytes 2359300
  148.4 1.4 copy-start.6
  148.4 1.4 copy-start.11
  152.2 2.0 copy-start.3
  156.7 47.2 %collective-permute-start = (bf16[256,1536]{1,0:T(8,128)(2,1)}, bf16[256,1536]{1,0:T(8,128)(2,1)S(1)}, u32[]{:S(2)}, u32[]{:S(2)}) collective-permute-start(bf16[256,1536]{1,0:T(8,128)(2,1)} %fusion.66), channel_id=1, source_target_pairs={{0,32},{32,64},{64,96},{96,128},{128,160},{160,192},{192,224},{224... | collective-permute-start | bytes 2359304 | tf_op jit(solution)/shard_map/ppermute | solution.py:105
  216.0 1.4 copy-start.1
  216.1 1.7 copy-start.5
  217.9 1.5 copy-start.14
  217.9 1.5 copy-start.15
  233.5 1.4 copy-start.2
  233.6 1.7 copy-start.7
  235.4 1.3 copy-start.10
